TPU v7x, 256 devices: a whole 4x4x8 slice. The times are simulated.
256 devices in a mesh: seq: 32 (over y, z_hi, core), head: 8 (over z_lo, x).
Axes of the slice: x: 4, y: 4, z: 8 (z_hi: 4, z_lo: 2; z = z_hi * 2 + z_lo), core: 2. Of those that a mesh axis runs over, the one named last changes fastest.
Arguments:
- xin: bfloat16 [16384, 8192], P('seq', 'head'), may hold values from -6 to 6
- gate_z: bfloat16 [16384, 8192], P('seq', 'head'), may hold values from -6 to 6
- b_proj: bfloat16 [16384, 8, 256], P('seq', 'head'), may hold values from -0.375 to 0.375
- c_proj: bfloat16 [16384, 8, 256], P('seq', 'head'), may hold values from -0.375 to 0.375
- log_retain: float32 [16384, 128], P('seq', 'head'), may hold values from -2 to 0, as said below
- skip_d: float32 [128], P('head'), may hold values from 0.5 to 2
- norm_gain: float32 [8192], P('head'), may hold values from 0.5 to 1.5
- w_out: bfloat16 [8192, 4096], P('head', 'seq'), may hold values from -0.0625 to 0.0625
- residual: bfloat16 [16384, 4096], P(('seq', 'head')), may hold values from -24 to 24
- refusal: float32 [4096], replicated, may hold values from -6 to 6
- stream_gain: float32 [4096], replicated, may hold values from 0.5 to 1.5
- w_in: bfloat16 [4096, 8192], P('seq', 'head'), may hold values from -0.09375 to 0.09375
Outputs:
- stream: bfloat16 [16384, 4096], P(('seq', 'head'))
- next_x: bfloat16 [16384, 8192], P('seq', 'head')
Inputs may be any that keep to these rules, and one draw needn't show every extreme that they name: `log_retain`: every entry is negative.
All inputs are finite; a program needn't handle non-finite values.
Results may differ from a plain program's by a relative error of at most 0.02.
Values may be sent and summed in bfloat16 or wider, within the bound.
No kernel may reach another device: no remote copies, remote signals or barrier semaphores. Data moves between devices by JAX's collectives and lax.ppermute only.
A program may use at most 192 MiB of HBM per device.

v0:
```python
import jax
import jax.numpy as jnp
from jax import lax
from jax.sharding import PartitionSpec as P

SPAN = 256


def prefix(array, axis, combine, identity):
    devices, place = (lax.axis_size(axis), lax.axis_index(axis))
    everything = jax.tree.map(
        lambda part, kind: lax.all_gather(part.astype(kind), axis),
        array,
        (jnp.bfloat16, jnp.bfloat16),
    )
    start = jax.tree.map(
        lambda part, zero: jnp.broadcast_to(jnp.asarray(zero, part.dtype), part.shape),
        array,
        identity,
    )

    def turn(k, before):
        reached = k < place
        new = combine(
            before, jax.tree.map(lambda part, own: part[k].astype(own.dtype), everything, array)
        )
        return jax.tree.map(lambda a, b: jnp.where(reached, a, b), new, before)

    return lax.fori_loop(0, devices, turn, start)


def carry_combine(earlier, later):
    decay_early, state_early = earlier
    decay_later, state_later = later
    return (
        decay_early + decay_later,
        jnp.exp(decay_later)[:, None, None] * state_early + state_later,
    )


def body(
    xin,
    gate_z,
    b_proj,
    c_proj,
    log_retain,
    skip_d,
    norm_gain,
    w_out,
    residual,
    refusal,
    stream_gain,
    w_in,
):
    seq_rows, channels = xin.shape
    head_count = log_retain.shape[1]
    head_width = channels // head_count
    group_count = b_proj.shape[1]
    state_width = b_proj.shape[2]
    per_group = head_count // group_count
    block_count = seq_rows // SPAN
    inputs = xin.reshape(block_count, SPAN, head_count, head_width)
    b_grouped = b_proj.reshape(block_count, SPAN, group_count, state_width)
    c_grouped = c_proj.reshape(block_count, SPAN, group_count, state_width)
    scores = jnp.einsum("klgn,ksgn->kgls", c_grouped, b_grouped, preferred_element_type=jnp.float32)
    scores = jnp.repeat(scores, per_group, axis=1)
    cum = jnp.cumsum(log_retain.reshape(block_count, SPAN, head_count), axis=1)
    cum_heads = jnp.transpose(cum, (0, 2, 1))
    later_pos = lax.broadcasted_iota(jnp.int32, (SPAN, SPAN), 0)
    earlier_pos = lax.broadcasted_iota(jnp.int32, (SPAN, SPAN), 1)
    causal = later_pos >= earlier_pos
    gap = cum_heads[:, :, :, None] - cum_heads[:, :, None, :]
    mixing = (jnp.where(causal, jnp.exp(jnp.where(causal, gap, 0.0)), 0.0) * scores).astype(
        jnp.bfloat16
    )
    intra = jnp.einsum("khls,kshp->klhp", mixing, inputs, preferred_element_type=jnp.float32)
    tail_decay = jnp.exp(cum_heads[:, :, -1:] - cum_heads)
    b_heads = jnp.repeat(b_grouped, per_group, axis=2)
    weighted_b = (
        b_heads.astype(jnp.float32) * jnp.transpose(tail_decay, (0, 2, 1))[..., None]
    ).astype(jnp.bfloat16)
    block_state = jnp.einsum(
        "klhn,klhp->khnp", weighted_b, inputs, preferred_element_type=jnp.float32
    )
    block_decay = cum_heads[:, :, -1]

    def advance(carried_state, pair):
        decay_here, state_here = pair
        return (jnp.exp(decay_here)[:, None, None] * carried_state + state_here, carried_state)

    zero_state = jnp.zeros((head_count, state_width, head_width), jnp.float32)
    device_state, local_starts = lax.scan(advance, zero_state, (block_decay, block_state))
    device_decay = jnp.sum(block_decay, axis=0)
    zero_decay = jnp.zeros((head_count,), jnp.float32)
    total_decay, incoming = prefix(
        (device_decay, device_state), "seq", carry_combine, (zero_decay, zero_state)
    )
    before_block = jnp.cumsum(block_decay, axis=0) - block_decay
    starts = local_starts + jnp.exp(before_block)[:, :, None, None] * incoming[None]
    c_heads = jnp.repeat(c_grouped, per_group, axis=2).astype(jnp.float32)
    carried = jnp.einsum("klhn,khnp->klhp", c_heads, starts, precision=lax.Precision.HIGHEST)
    carried = carried * jnp.exp(cum)[..., None]
    mixed = intra + carried + skip_d[None, None, :, None] * inputs.astype(jnp.float32)
    gated = mixed * jax.nn.silu(
        gate_z.reshape(block_count, SPAN, head_count, head_width).astype(jnp.float32)
    )
    grouped = gated.reshape(seq_rows, group_count, per_group * head_width)
    grouped = grouped * lax.rsqrt(jnp.mean(grouped * grouped, axis=-1, keepdims=True) + 1e-05)
    ssd_out = (grouped.reshape(seq_rows, channels) * norm_gain[None, :]).astype(jnp.bfloat16)
    partial_sum = jnp.dot(
        ssd_out,
        lax.all_gather(w_out, "seq", axis=1, tiled=True),
        preferred_element_type=jnp.float32,
    )
    mixer_out = lax.psum_scatter(
        partial_sum.astype(jnp.bfloat16), "head", scatter_dimension=0, tiled=True
    ).astype(jnp.float32)
    unit = refusal / jnp.sqrt(jnp.sum(refusal * refusal) + 1e-06)
    hidden = residual.astype(jnp.float32) + mixer_out
    coef = jnp.dot(hidden, unit, precision=lax.Precision.HIGHEST)
    stream = (hidden - coef[:, None] * unit[None, :]).astype(jnp.bfloat16)
    stream_float = stream.astype(jnp.float32)
    normed = (
        stream_float
        * lax.rsqrt(jnp.mean(stream_float * stream_float, axis=-1, keepdims=True) + 1e-05)
        * stream_gain[None, :]
    ).astype(jnp.bfloat16)
    all_rows = lax.all_gather(normed, "head", axis=0, tiled=True)
    next_float = jnp.dot(
        all_rows,
        lax.all_gather(w_in, "seq", axis=0, tiled=True),
        preferred_element_type=jnp.float32,
    )
    return (stream, next_float.astype(jnp.bfloat16))


def solution(mesh):
    in_specs = (
        P("seq", "head"),
        P("seq", "head"),
        P("seq", "head", None),
        P("seq", "head", None),
        P("seq", "head"),
        P("head"),
        P("head"),
        P("head", "seq"),
        P(("seq", "head"), None),
        P(),
        P(),
        P("seq", "head"),
    )
    out_specs = (P(("seq", "head"), None), P("seq", "head"))
    return jax.shard_map(body, mesh=mesh, in_specs=in_specs, out_specs=out_specs, check_vma=False)
```

profile of v0, /device:TPU:1, one launch (start us, length us, event | category | flops | bytes accessed | tf_op | source)
XLA Modules:
  0.0 529.7 jit_solution(17022700494069063450)
XLA Ops:
  10.4 4.0 reshape.182
  14.4 2.8 copy.50
  17.2 2.0 convert_element_type.84
  19.1 5.1 fusion.4
  24.2 6.9 %while.27 = (s32[]{:T(128)}, f32[16,256,64]{2,1,0:T(8,128)S(1)}, f32[2,16,256,64]{3,2,1,0:T(8,128)}, f32[2,16]{1,0:T(2,128)S(1)}, f32[2,16,256,64]{3,2,1,0:T(8,128)}, /*index=5*/s32[]{:T(128)}, s32[]{:T(128)}) while((s32[]{:T(128)}, f32[16,256,64]{2,1,0:T(8,128)S(1)}, f32[2,16,256,64]{3,2,1,0:T(8,128)}, f32[2,16]{1,0:T(2,128)S(1)}, ...), condition=%wide.region_3.4_spmd.clone, body=%wide.region_2.3_spmd.clone.sunk | while | flops 1048579 | bytes 14680892 | solution.py:92
  34.7 76.6 %all-reduce = bf16[512]{0:T(512)(128)(2,1)S(1)} all-reduce(bf16[512]{0:T(512)(128)(2,1)S(1)} %dynamic-update-slice), channel_id=2, replica_groups=mesh['seq'=32,'head'=8] {'seq'}, use_global_device_ids=true, to_apply=%add | all-reduce | flops 512 | bytes 2048
  111.4 2.0 fusion.27
  113.4 2.6 reshape.183
  116.0 4.6 copy.59
  120.6 25.5 %all-gather.13.cloned.1.call-done = bf16[512,256,64]{1,2,0:T(8,128)(2,1)} async-done(((bf16[16,256,64]{1,2,0:T(8,128)(2,1)}), bf16[512,256,64]{1,2,0:T(8,128)(2,1)}) %all-gather.13.cloned.1.call-update) | async-done | bytes 16777232 | tf_op jit(solution)/shard_map/all_gather | solution.py:12
  146.1 144.1 %while.28 = (s32[]{:T(128)}, f32[16,256,64]{2,1,0:T(8,128)S(1)}, s32[]{:T(128)}, bf16[32,16]{1,0:T(8,128)(2,1)S(1)}, bf16[32,16,256,64]{2,3,1,0:T(8,128)(2,1)}, /*index=5*/s32[]{:T(128)}, s32[]{:T(128)}) while((s32[]{:T(128)}, f32[16,256,64]{2,1,0:T(8,128)S(1)}, s32[]{:T(128)}, bf16[32,16]{1,0:T(8,128)(2,1)S(1)}, ...), condition=%wide.region_7.8_spmd.clone, body=%wide.region_6.7_spmd.clone.sunk | while | flops 1310740 | bytes 4718857 | solution.py:29
  150.6 1.9 constant_dynamic-slice_fusion.3
  159.6 1.9 constant_dynamic-slice_fusion.3
  164.1 1.9 constant_dynamic-slice_fusion.3
  168.5 1.9 constant_dynamic-slice_fusion.3
  173.1 1.9 constant_dynamic-slice_fusion.3
  177.6 1.9 constant_dynamic-slice_fusion.3
  182.1 1.9 constant_dynamic-slice_fusion.3
  186.6 1.9 constant_dynamic-slice_fusion.3
  191.1 1.9 constant_dynamic-slice_fusion.3
  195.5 1.9 constant_dynamic-slice_fusion.3
  200.1 1.9 constant_dynamic-slice_fusion.3
  213.5 1.9 constant_dynamic-slice_fusion.3
  227.0 2.0 constant_dynamic-slice_fusion.3
  290.3 6.0 %fusion.5 = f32[2,16,64,256]{3,2,1,0:T(8,128)S(1)} fusion(f32[2,16,256,64]{3,2,1,0:T(8,128)} %get-tuple-element.124, bf16[2,256,256]{2,1,0:T(8,128)(2,1)S(1)} %bitcast.79, f32[16,256,64]{2,1,0:T(8,128)S(1)} %get-tuple-element.126, f32[2,16]{1,0:T(2,128)S(1)} %subtract_exponential_fusion), kind=kOutput, calls=%fused_computation.14 | convolution fusion | flops 1611661312 | bytes 5505152 | tf_op jit(solution)/shard_map/klhn,khnp->klhp/dot_general | solution.py:101
  296.4 3.0 multiply_reduce_fusion
  302.6 10.9 %convolution_convert_fusion = bf16[512,4096]{1,0:T(8,128)(2,1)} fusion(bf16[1024,4096]{1,0:T(8,128)(2,1)} %all-gather.7.cloned.1.call-done, f32[512,1024]{0,1:T(8,128)} %bitcast.81, f32[1024]{0:T(1024)S(1)} %copy-done.13, f32[512]{0:T(512)S(1)} %bitcast.87), kind=kOutput, calls=%fused_computation.11 | convolution fusion | flops 4298637312 | bytes 14686208 | tf_op jit(solution)/shard_map/dot_general | solution.py:110
  315.6 61.8 %reduce-scatter.2.cloned.1.call-done = bf16[64,4096]{1,0:T(8,128)(2,1)} async-done(((bf16[512,4096]{1,0:T(8,128)(2,1)}), bf16[64,4096]{1,0:T(8,128)(2,1)}) %reduce-scatter.2.cloned.1.call-update) | async-done | bytes 524304 | tf_op jit(solution)/shard_map/reduce_scatter | solution.py:115
  377.4 2.0 convolution_bitcast_fusion
  381.8 73.2 %all-gather.11.cloned.1.call-done = bf16[4096,1024]{1,0:T(8,128)(2,1)} async-done(((bf16[128,1024]{1,0:T(8,128)(2,1)}), bf16[4096,1024]{1,0:T(8,128)(2,1)}) %all-gather.11.cloned.1.call-update) | async-done | bytes 8388624 | tf_op jit(solution)/shard_map/all_gather | solution.py:131
  455.0 57.9 %all-gather.9.cloned.1.call-done = bf16[512,4096]{1,0:T(8,128)(2,1)} async-done(((bf16[64,4096]{1,0:T(8,128)(2,1)}), bf16[512,4096]{1,0:T(8,128)(2,1)}) %all-gather.9.cloned.1.call-update) | async-done | bytes 4194320 | tf_op jit(solution)/shard_map/all_gather | solution.py:128
  513.0 10.1 %convolution_convert_fusion.1 = bf16[512,1024]{1,0:T(8,128)(2,1)} fusion(bf16[512,4096]{1,0:T(8,128)(2,1)} %all-gather.9.cloned.1.call-done, bf16[4096,1024]{1,0:T(8,128)(2,1)} %all-gather.11.cloned.1.call-done), kind=kOutput, calls=%fused_computation.33 | convolution fusion | flops 4295491584 | bytes 13631488 | tf_op jit(solution)/shard_map/dot_general | solution.py:129
  (194 shorter events, 137.8 us)
Async XLA Ops:
  7.2 104.2 %copy-start = (bf16[512,1,256]{2,0,1:T(8,128)(2,1)S(1)}, bf16[512,1,256]{2,0,1:T(8,128)(2,1)}, u32[]{:S(2)}) copy-start(bf16[512,1,256]{2,0,1:T(8,128)(2,1)} %param.19) | copy-start | bytes 786436
  7.2 138.9 %all-gather.13.cloned.1.call-start = ((), (), s32[]{:S(2)}) async-start(), calls=%async_computation.5 | async-start | bytes 17301504 | tf_op jit(solution)/shard_map/all_gather | solution.py:12
  17.2 7.1 %copy-start.3 = (bf16[2,256,16,64]{1,3,2,0:T(8,128)(2,1)}, bf16[2,256,16,64]{1,3,2,0:T(8,128)(2,1)S(1)}, u32[]{:S(2)}) copy-start(bf16[2,256,16,64]{1,3,2,0:T(8,128)(2,1)S(1)} %copy.50) | copy-start | bytes 3145732
  24.2 2.9 copy-start.2
  27.7 2.9 copy-start.2
  31.2 2.1 copy-start.15
  31.2 82.2 %copy-start.8 = (bf16[512,1024]{1,0:T(8,128)(2,1)S(1)}, bf16[512,1024]{1,0:T(8,128)(2,1)}, u32[]{:S(2)}) copy-start(bf16[512,1024]{1,0:T(8,128)(2,1)} %param.17) | copy-start | bytes 3145732
  32.3 270.3 %all-gather.7.cloned.1.call-start = ((), (), s32[]{:S(2)}) async-start(), calls=%async_computation.1 | async-start | bytes 8650752 | tf_op jit(solution)/shard_map/all_gather | solution.py:112
  33.1 344.3 %reduce-scatter.2.cloned.1.call-start = ((), (), s32[]{:S(2)}) async-start(), calls=%async_computation.2 | async-start | bytes 4718592 | tf_op jit(solution)/shard_map/reduce_scatter | solution.py:115
  290.2 6.1 %copy-start.4 = (bf16[2,256,16,64]{1,3,2,0:T(8,128)(2,1)S(1)}, bf16[2,256,16,64]{1,3,2,0:T(8,128)(2,1)}, u32[]{:S(2)}) copy-start(bf16[2,256,16,64]{1,3,2,0:T(8,128)(2,1)} %copy-done.3) | copy-start | bytes 3145732
  290.2 6.1 %copy-start.5 = (f32[2,256,16,64]{1,3,2,0:T(8,128)S(1)}, f32[2,256,16,64]{1,3,2,0:T(8,128)}, u32[]{:S(2)}) copy-start(f32[2,256,16,64]{1,3,2,0:T(8,128)} %copy.59) | copy-start | bytes 6291460
  290.2 6.1 %copy-start.9 = (f32[2,256,256]{2,1,0:T(8,128)S(1)}, f32[2,256,256]{2,1,0:T(8,128)}, u32[]{:S(2)}) copy-start(f32[2,256,256]{2,1,0:T(8,128)} %fusion.27) | copy-start | bytes 1572868
  290.2 6.1 %copy-start.11 = (f32[2,256,16]{1,2,0:T(8,128)S(1)}, f32[2,256,16]{1,2,0:T(8,128)}, u32[]{:S(2)}) copy-start(f32[2,256,16]{1,2,0:T(8,128)} %get-tuple-element.212) | copy-start | bytes 98308
  290.3 6.1 %copy-start.14 = (f32[16]{0:T(128)S(1)}, f32[16]{0:T(128)}, u32[]{:S(2)}) copy-start(f32[16]{0:T(128)} %param.21) | copy-start | bytes 196
  301.1 1.6 copy-start.13
  313.5 0.7 copy-start.10
  313.5 63.8 %copy-start.6 = (bf16[64,4096]{1,0:T(8,128)(2,1)S(1)}, bf16[64,4096]{1,0:T(8,128)(2,1)}, u32[]{:S(2)}) copy-start(bf16[64,4096]{1,0:T(8,128)(2,1)} %param.24) | copy-start | bytes 1572868
  313.6 67.2 %copy-start.12 = (f32[4096]{0:T(1024)S(1)}, f32[4096]{0:T(1024)}, u32[]{:S(2)}) copy-start(f32[4096]{0:T(1024)} %param.26) | copy-start | bytes 49156
  313.6 141.4 %all-gather.11.cloned.1.call-start = ((), (), s32[]{:S(2)}) async-start(), calls=%async_computation.4 | async-start | bytes 8650752 | tf_op jit(solution)/shard_map/all_gather | solution.py:131
  314.2 198.8 %all-gather.9.cloned.1.call-start = ((), (), s32[]{:S(2)}) async-start(), calls=%async_computation.3 | async-start | bytes 4718592 | tf_op jit(solution)/shard_map/all_gather | solution.py:128
  380.8 142.3 %copy-start.7 = (bf16[64,4096]{1,0:T(8,128)(2,1)}, bf16[64,4096]{1,0:T(8,128)(2,1)S(1)}, u32[]{:S(2)}) copy-start(bf16[64,4096]{1,0:T(8,128)(2,1)S(1)} %get-tuple-element.211) | copy-start | bytes 1572868
  513.0 10.2 %copy-start.1 = (bf16[512,1,256]{2,0,1:T(8,128)(2,1)S(1)}, bf16[512,1,256]{2,0,1:T(8,128)(2,1)}, u32[]{:S(2)}) copy-start(bf16[512,1,256]{2,0,1:T(8,128)(2,1)} %param.19) | copy-start | bytes 786436
Sparse Core Ops, SparseCore 0:
  32.5 113.5 all-gather.12
  148.6 93.9 all-gather.6
  313.7 63.6 reduce-scatter.1
  379.8 75.2 all-gather.10
  457.2 55.6 all-gather.8
where the time goes:
time: 533 us; the launch traced here: 530 us
  waiting for transfers between devices  220 us (41%)
  local copies, waits for them, and re-layouts  132 us (25%)
  blocking collectives  76.6 us (14%)
  other arithmetic  44.8 us (8%)
  matrix products  39.3 us (7%)
  between operations  15.4 us (3%)
    dynamic_slice x64, local copies, waits for them, and re-layouts, turn(): part[k].astype(own.dtype)  109 us
    unnamed x1, blocking collectives  76.6 us
    all_gather x1, waiting for transfers between devices, body(): lax.all_gather(w_in, 'seq', axis=0, tiled=True)  73.2 us
    reduce_scatter x1, waiting for transfers between devices, body(): lax.psum_scatter(partial_sum.astype(jnp.bfloat16), 'head', scatter_dimens...  61.8 us
    all_gather x1, waiting for transfers between devices, body(): all_rows = lax.all_gather(normed, 'head', axis=0, tiled=True)  57.9 us
    select_n x32, other arithmetic, turn(): return jax.tree.map(lambda a, b: jnp.where(reached, a, b), new, before)  33 us
    all_gather x1, waiting for transfers between devices, prefix(): lax.all_gather(part.astype(kind), axis)  25.5 us
    dot_general x1, matrix products, body(): jnp.dot(ssd_out, lax.all_gather(w_out, 'seq', axis=1, tiled=True), prefer...  10.9 us
  transfers between devices with their start and end apart: 5, of which 4 were waited for; matrix products, arithmetic and copies ran while one was open for 32% of the time, Pallas kernels for 0%

commit v1 on v0

--- a/solution.py
+++ b/solution.py
@@ -126,11 +126,10 @@
         * stream_gain[None, :]
     ).astype(jnp.bfloat16)
     all_rows = lax.all_gather(normed, "head", axis=0, tiled=True)
-    next_float = jnp.dot(
-        all_rows,
-        lax.all_gather(w_in, "seq", axis=0, tiled=True),
-        preferred_element_type=jnp.float32,
+    put_face = lambda z: jnp.concatenate(
+        lax.all_to_all(jnp.stack([z for _ in range(lax.axis_size("seq"))]), "seq", 0, 0), 0
     )
+    next_float = jnp.dot(all_rows, put_face(w_in), preferred_element_type=jnp.float32)
     return (stream, next_float.astype(jnp.bfloat16))
 
 

time: 533 us -> 617 us (1.16)
  waiting for transfers between devices: 220 us -> 281 us
  starting transfers between devices: 0.2 us -> 19.5 us
    all_to_all x0 -> x1, waiting for transfers between devices: none -> 120 us  [body(): lax.all_to_all(jnp.stack([z for _ in range(lax.axis_size('seq'))]), 'seq'...]
    reduce_scatter x1, waiting for transfers between devices: 61.8 us -> 137 us  [body(): lax.psum_scatter(partial_sum.astype(jnp.bfloat16), 'head', scatter_dimens...]
    all_gather x1 -> x0, waiting for transfers between devices: 73.2 us -> none  [body(): lax.all_gather(w_in, 'seq', axis=0, tiled=True)]
    all_gather x1, waiting for transfers between devices: 57.9 us -> 0.01 us  [body(): all_rows = lax.all_gather(normed, 'head', axis=0, tiled=True)]
    all_to_all x0 -> x1, starting transfers between devices: none -> 19.3 us  [body(): lax.all_to_all(jnp.stack([z for _ in range(lax.axis_size('seq'))]), 'seq'...]
  transfers between devices with their start and end apart: 5 -> 5, of which waited for: 4 -> 3; matrix products, arithmetic and copies ran while one was open for 32% -> 28% of each run, Pallas kernels for 0% -> 0%
where the time goes in v1:
time: 617 us; the launch traced here: 613 us
  waiting for transfers between devices  281 us (46%)
  local copies, waits for them, and re-layouts  136 us (22%)
  blocking collectives  76.5 us (12%)
  other arithmetic  44.7 us (7%)
  matrix products  38 us (6%)
  starting transfers between devices  19.5 us (3%)
  between operations  15.4 us (2%)
    reduce_scatter x1, waiting for transfers between devices, body(): lax.psum_scatter(partial_sum.astype(jnp.bfloat16), 'head', scatter_dimens...  137 us
    all_to_all x1, waiting for transfers between devices, body(): lax.all_to_all(jnp.stack([z for _ in range(lax.axis_size('seq'))]), 'seq'...  120 us
    dynamic_slice x64, local copies, waits for them, and re-layouts, turn(): part[k].astype(own.dtype)  109 us
    unnamed x1, blocking collectives  76.5 us
    select_n x32, other arithmetic, turn(): return jax.tree.map(lambda a, b: jnp.where(reached, a, b), new, before)  33 us
    all_gather x1, waiting for transfers between devices, prefix(): lax.all_gather(part.astype(kind), axis)  23.4 us
    all_to_all x1, starting transfers between devices, body(): lax.all_to_all(jnp.stack([z for _ in range(lax.axis_size('seq'))]), 'seq'...  19.3 us
  transfers between devices with their start and end apart: 5, of which 3 were waited for; matrix products, arithmetic and copies ran while one was open for 28% of the time, Pallas kernels for 0%

profile of v1, /device:TPU:1, one launch (start us, length us, event | category | flops | bytes accessed | tf_op | source)
XLA Modules:
  0.0 612.7 jit_solution(16178177677445454261)
XLA Ops:
  10.4 4.0 reshape.188
  14.4 2.8 copy.50
  17.2 2.0 convert_element_type.84
  19.1 5.1 fusion.4
  24.2 6.9 %while.27 = (s32[]{:T(128)}, f32[16,256,64]{2,1,0:T(8,128)S(1)}, f32[2,16,256,64]{3,2,1,0:T(8,128)}, f32[2,16]{1,0:T(2,128)S(1)}, f32[2,16,256,64]{3,2,1,0:T(8,128)}, /*index=5*/s32[]{:T(128)}, s32[]{:T(128)}) while((s32[]{:T(128)}, f32[16,256,64]{2,1,0:T(8,128)S(1)}, f32[2,16,256,64]{3,2,1,0:T(8,128)}, f32[2,16]{1,0:T(2,128)S(1)}, ...), condition=%wide.region_3.4_spmd.clone, body=%wide.region_2.3_spmd.clone.sunk | while | flops 1048579 | bytes 14680892 | solution.py:92
  34.7 76.5 %all-reduce = bf16[512]{0:T(512)(128)(2,1)S(1)} all-reduce(bf16[512]{0:T(512)(128)(2,1)S(1)} %dynamic-update-slice), channel_id=2, replica_groups=mesh['seq'=32,'head'=8] {'seq'}, use_global_device_ids=true, to_apply=%add | all-reduce | flops 512 | bytes 2048
  111.4 2.0 fusion.27
  113.4 2.6 reshape.189
  116.0 4.6 copy.59
  120.6 23.4 %all-gather.10.cloned.1.call-done = bf16[512,256,64]{1,2,0:T(8,128)(2,1)} async-done(((bf16[16,256,64]{1,2,0:T(8,128)(2,1)}), bf16[512,256,64]{1,2,0:T(8,128)(2,1)}) %all-gather.10.cloned.1.call-update) | async-done | bytes 16777232 | tf_op jit(solution)/shard_map/all_gather | solution.py:12
  143.9 143.8 %while.28 = (s32[]{:T(128)}, f32[16,256,64]{2,1,0:T(8,128)S(1)}, s32[]{:T(128)}, bf16[32,16]{1,0:T(8,128)(2,1)S(1)}, bf16[32,16,256,64]{2,3,1,0:T(8,128)(2,1)}, /*index=5*/s32[]{:T(128)}, s32[]{:T(128)}) while((s32[]{:T(128)}, f32[16,256,64]{2,1,0:T(8,128)S(1)}, s32[]{:T(128)}, bf16[32,16]{1,0:T(8,128)(2,1)S(1)}, ...), condition=%wide.region_7.8_spmd.clone, body=%wide.region_6.7_spmd.clone.sunk | while | flops 1310740 | bytes 4718857 | solution.py:29
  148.4 1.9 constant_dynamic-slice_fusion.3
  152.9 1.9 constant_dynamic-slice_fusion.3
  157.4 1.9 constant_dynamic-slice_fusion.3
  161.9 1.9 constant_dynamic-slice_fusion.3
  166.4 1.9 constant_dynamic-slice_fusion.3
  170.9 1.9 constant_dynamic-slice_fusion.3
  175.4 1.9 constant_dynamic-slice_fusion.3
  184.4 1.9 constant_dynamic-slice_fusion.3
  188.9 1.9 constant_dynamic-slice_fusion.3
  197.8 1.9 constant_dynamic-slice_fusion.3
  211.3 1.9 constant_dynamic-slice_fusion.3
  229.3 1.9 constant_dynamic-slice_fusion.3
  287.8 6.0 fusion.5
  293.9 3.0 multiply_reduce_fusion
  299.3 9.7 %convolution_convert_fusion = bf16[512,4096]{1,0:T(8,128)(2,1)} fusion(bf16[1024,4096]{1,0:T(8,128)(2,1)} %all-gather.6.cloned.1.call-done, f32[512,1024]{0,1:T(8,128)S(1)} %bitcast.82, f32[1024]{0:T(1024)S(1)} %copy-done.14, f32[512]{0:T(512)S(1)} %bitcast.88), kind=kOutput, calls=%fused_computation.11 | convolution fusion | flops 4298637312 | bytes 14686208 | tf_op jit(solution)/shard_map/dot_general | solution.py:110
  309.9 4.3 stack.2
  314.2 19.3 %all-to-all-start = ((bf16[32,128,1024]{2,1,0:T(8,128)(2,1)}), bf16[32,128,1024]{2,1,0:T(8,128)(2,1)}, u32[]{:S(2)}, u32[]{:S(2)}) async-start(bf16[32,128,1024]{2,1,0:T(8,128)(2,1)} %stack.2), calls=%async_computation.1 | async-start | bytes 16777216 | tf_op jit(solution)/shard_map/all_to_all | solution.py:130
  334.9 137.1 %reduce-scatter.2.cloned.1.call-done = bf16[64,4096]{1,0:T(8,128)(2,1)} async-done(((bf16[512,4096]{1,0:T(8,128)(2,1)}), bf16[64,4096]{1,0:T(8,128)(2,1)}) %reduce-scatter.2.cloned.1.call-update) | async-done | bytes 524304 | tf_op jit(solution)/shard_map/reduce_scatter | solution.py:115
  472.0 2.0 convolution_bitcast_fusion
  476.4 119.5 %all-to-all-done = bf16[32,128,1024]{2,1,0:T(8,128)(2,1)} async-done(((bf16[32,128,1024]{2,1,0:T(8,128)(2,1)}), bf16[32,128,1024]{2,1,0:T(8,128)(2,1)}, u32[]{:S(2)}, u32[]{:S(2)}) %all-to-all-start) | async-done | bytes 8388640 | tf_op jit(solution)/shard_map/all_to_all | solution.py:130
  596.0 10.2 %convolution_convert_fusion.1 = bf16[512,1024]{1,0:T(8,128)(2,1)} fusion(bf16[512,4096]{1,0:T(8,128)(2,1)} %all-gather.8.cloned.1.call-done, bf16[4096,1024]{1,0:T(8,128)(2,1)} %bitcast.11), kind=kOutput, calls=%fused_computation.33 | convolution fusion | flops 4295491584 | bytes 13631488 | tf_op jit(solution)/shard_map/dot_general | solution.py:132
  (196 shorter events, 139.2 us)
Async XLA Ops:
  7.2 104.2 %copy-start = (bf16[512,1,256]{2,0,1:T(8,128)(2,1)S(1)}, bf16[512,1,256]{2,0,1:T(8,128)(2,1)}, u32[]{:S(2)}) copy-start(bf16[512,1,256]{2,0,1:T(8,128)(2,1)} %param.19) | copy-start | bytes 786436
  7.2 136.8 %all-gather.10.cloned.1.call-start = ((), (), s32[]{:S(2)}) async-start(), calls=%async_computation.5 | async-start | bytes 17301504 | tf_op jit(solution)/shard_map/all_gather | solution.py:12
  17.2 7.1 %copy-start.3 = (bf16[2,256,16,64]{1,3,2,0:T(8,128)(2,1)}, bf16[2,256,16,64]{1,3,2,0:T(8,128)(2,1)S(1)}, u32[]{:S(2)}) copy-start(bf16[2,256,16,64]{1,3,2,0:T(8,128)(2,1)S(1)} %copy.50) | copy-start | bytes 3145732
  24.2 2.9 copy-start.2
  27.7 2.9 copy-start.2
  31.2 2.1 copy-start.16
  31.2 82.2 %copy-start.8 = (bf16[512,1024]{1,0:T(8,128)(2,1)S(1)}, bf16[512,1024]{1,0:T(8,128)(2,1)}, u32[]{:S(2)}) copy-start(bf16[512,1024]{1,0:T(8,128)(2,1)} %param.17) | copy-start | bytes 3145732
  32.3 266.5 %all-gather.6.cloned.1.call-start = ((), (), s32[]{:S(2)}) async-start(), calls=%async_computation.2 | async-start | bytes 8650752 | tf_op jit(solution)/shard_map/all_gather | solution.py:112
  33.1 438.9 %reduce-scatter.2.cloned.1.call-start = ((), (), s32[]{:S(2)}) async-start(), calls=%async_computation.3 | async-start | bytes 4718592 | tf_op jit(solution)/shard_map/reduce_scatter | solution.py:115
  287.7 6.1 copy-start.4
  287.7 6.1 copy-start.5
  287.8 6.1 copy-start.9
  287.8 6.1 copy-start.12
  287.8 6.1 copy-start.15
  298.6 0.7 copy-start.14
  308.9 0.9 copy-start.10
  314.2 19.4 %copy-start.11 = (f32[4096]{0:T(1024)S(1)}, f32[4096]{0:T(1024)}, u32[]{:S(2)}) copy-start(f32[4096]{0:T(1024)} %param.25) | copy-start | bytes 49156
  314.2 157.8 %copy-start.6 = (bf16[64,4096]{1,0:T(8,128)(2,1)S(1)}, bf16[64,4096]{1,0:T(8,128)(2,1)}, u32[]{:S(2)}) copy-start(bf16[64,4096]{1,0:T(8,128)(2,1)} %param.24) | copy-start | bytes 1572868
  314.2 281.8 %all-to-all-start = ((bf16[32,128,1024]{2,1,0:T(8,128)(2,1)}), bf16[32,128,1024]{2,1,0:T(8,128)(2,1)}, u32[]{:S(2)}, u32[]{:S(2)}) async-start(bf16[32,128,1024]{2,1,0:T(8,128)(2,1)} %stack.2), calls=%async_computation.1 | async-start | bytes 16777216 | tf_op jit(solution)/shard_map/all_to_all | solution.py:130
  333.5 141.9 %copy-start.13 = (f32[4096]{0:T(1024)S(1)}, f32[4096]{0:T(1024)}, u32[]{:S(2)}) copy-start(f32[4096]{0:T(1024)} %param.26) | copy-start | bytes 49156
  333.5 262.4 %all-gather.8.cloned.1.call-start = ((), (), s32[]{:S(2)}) async-start(), calls=%async_computation.4 | async-start | bytes 4718592 | tf_op jit(solution)/shard_map/all_gather | solution.py:128
  475.4 130.7 %copy-start.7 = (bf16[64,4096]{1,0:T(8,128)(2,1)}, bf16[64,4096]{1,0:T(8,128)(2,1)S(1)}, u32[]{:S(2)}) copy-start(bf16[64,4096]{1,0:T(8,128)(2,1)S(1)} %get-tuple-element.211) | copy-start | bytes 1572868
  596.0 10.2 %copy-start.1 = (bf16[512,1,256]{2,0,1:T(8,128)(2,1)S(1)}, bf16[512,1,256]{2,0,1:T(8,128)(2,1)}, u32[]{:S(2)}) copy-start(bf16[512,1,256]{2,0,1:T(8,128)(2,1)} %param.19) | copy-start | bytes 786436
Sparse Core Ops, SparseCore 0:
  32.5 111.4 all-gather.9
  146.4 96.5 all-gather.5
  309.1 162.8 reduce-scatter.1
  476.6 117.5 all-gather.7
